TPU v7x, 256 devices: a whole 4x4x8 slice. The times are simulated.
256 devices in a mesh: tok: 32 (over x, z), head: 8 (over y, core).
Axes of the slice: x: 4, y: 4, z: 8, core: 2. Of those that a mesh axis runs over, the one named last changes fastest.
Arguments:
- tokens: bfloat16 [32768, 1664], P(('tok', 'head')), may hold values from -75 to 75
- attn_gain: float32 [1664], replicated, may hold values from 0.1 to 1.9
- qkv_weight: bfloat16 [3, 1664, 1664], P(None, 'head'), may hold values from -5 to 5
- out_weight: bfloat16 [1664, 1664], P('head'), may hold values from -0.4375 to 0.4375
- merge_gain: float32 [1664], replicated, may hold values from 0.1 to 1.9
- merge_weight: bfloat16 [6656, 4096], P('head', 'tok'), may hold values from -0.078125 to 0.078125
- grid_sizes: int32 [2, 128], P(None, 'tok'), may hold values from 2 to 16, as said below
- segment_ids: int32 [32768], P('tok'), may hold values from 0 to 127, as said below
- patch_pos: int32 [2, 32768], P(None, 'tok'), may hold values from 0 to 15, as said below
- live_mask: int32 [32768], P('tok'), may hold values from 0 to 1, as said below
- owners: int32 [8192, 1], P(('tok', 'head')), may hold values from 0 to 31; in each aligned block of 32 rows (0 to 31, 32 to 63, ...) at most 2 rows name the same one
Outputs:
- delivered: bfloat16 [16384, 4096], P(('tok', 'head'))
Inputs may be any that keep to these rules, and one draw needn't show every extreme that they name: `grid_sizes`: both sides of every image are even, and some image is 16 by 16. `segment_ids`: never fall along the tokens. The aligned block b of 1024 tokens holds images b * 4 to (b + 1) * 4 - 1 packed in order from the block's start, image s taking grid_sizes[0, s] * grid_sizes[1, s] tokens; the block's remaining tokens carry the number of its last image. `patch_pos`: an image's tokens come in 2x2 windows, windows in row-major order, each window as (2 * r, 2 * c), (2 * r, 2 * c + 1), (2 * r + 1, 2 * c), (2 * r + 1, 2 * c + 1); padding tokens sit at (0, 0). `live_mask`: 1 exactly on the tokens that belong to an image. `owners`: in each aligned block of 32 rows (the merged rows of one device) no owner is named more than 2 times.
All inputs are finite; a program needn't handle non-finite values.
Results may differ from a plain program's by a relative error of at most 0.024.
Values may be sent and summed in bfloat16 or wider, within the bound.
No kernel may reach another device: no remote copies, remote signals or barrier semaphores. Data moves between devices by JAX's collectives and lax.ppermute only.
A program may use at most 64 MiB of HBM per device.

v0:
```python
import jax
import jax.numpy as jnp
from jax import lax
from jax.sharding import PartitionSpec as P

D = 1664
HD = 104
SIDE = 16
EPSILON = 1e-06
NEGATIVE = -1e30


def layer_norm(values, gain_vec):
    average = jnp.mean(values, axis=-1, keepdims=True)
    centred = values - average
    variance = jnp.mean(centred * centred, axis=-1, keepdims=True)
    return centred * lax.rsqrt(variance + EPSILON) * gain_vec


def rotate(vectors, row_coord, col_coord):
    quarter = vectors.shape[-1] // 4
    frequency = 10000.0 ** (-jnp.arange(quarter, dtype=jnp.float32) / quarter)
    pieces = []
    for which_axis, coordinate in ((0, row_coord), (1, col_coord)):
        leading = vectors[..., 2 * which_axis * quarter : (2 * which_axis + 1) * quarter]
        trailing = vectors[..., (2 * which_axis + 1) * quarter : (2 * which_axis + 2) * quarter]
        angles = coordinate[:, None, None] * frequency
        cosine = jnp.cos(angles)
        sine_val = jnp.sin(angles)
        pieces.append(leading * cosine - trailing * sine_val)
        pieces.append(leading * sine_val + trailing * cosine)
    return jnp.concatenate(pieces, axis=-1)


def body(
    tokens,
    attn_gain,
    qkv_weight,
    out_weight,
    merge_gain,
    merge_weight,
    grid_sizes,
    segment_ids,
    patch_pos,
    live_mask,
    owners,
):
    group_len = segment_ids.shape[0]
    local_rows = tokens.shape[0]
    head_width = qkv_weight.shape[1]
    heads_here = head_width // HD
    tok_count = lax.axis_size("tok")
    image_count = grid_sizes.shape[1]
    local_image = segment_ids - lax.axis_index("tok") * image_count
    image_match = local_image[:, None] == jnp.arange(image_count, dtype=jnp.int32)[None, :]
    grid_float = grid_sizes.astype(jnp.float32)
    row_size = jnp.sum(jnp.where(image_match, grid_float[0][None, :], 0.0), axis=1)
    col_size = jnp.sum(jnp.where(image_match, grid_float[1][None, :], 0.0), axis=1)
    row_coord = patch_pos[0].astype(jnp.float32) * SIDE / row_size
    col_coord = patch_pos[1].astype(jnp.float32) * SIDE / col_size
    stacked_weight = qkv_weight.reshape(3 * head_width, D)
    normed = layer_norm(tokens.astype(jnp.float32), attn_gain).astype(jnp.bfloat16)
    projected_rows = lax.dot_general(
        lax.all_gather(normed, "head", axis=0, tiled=True),
        stacked_weight,
        (((1,), (1,)), ((), ())),
        preferred_element_type=jnp.float32,
    )
    projected_rows = projected_rows.reshape(group_len, 3, heads_here, HD)
    query_all = (rotate(projected_rows[:, 0], row_coord, col_coord) * HD ** (-0.5)).astype(
        jnp.bfloat16
    )
    key_all = rotate(projected_rows[:, 1], row_coord, col_coord).astype(jnp.bfloat16)
    value_all = projected_rows[:, 2].astype(jnp.bfloat16)
    block_len = min(512, group_len)
    block_count = group_len // block_len
    key_live = live_mask == 1

    def allowed_pairs(query_start, span):
        query_seg = lax.dynamic_slice_in_dim(segment_ids, query_start, block_len)
        query_place = query_start + jnp.arange(block_len, dtype=jnp.int32)
        key_place = jnp.arange(span, dtype=jnp.int32)
        same_image = query_seg[:, None] == segment_ids[None, :]
        return same_image & (key_live[None, :] | (query_place[:, None] == key_place[None, :]))

    def query_block(query_start):
        queries = lax.dynamic_slice_in_dim(query_all, query_start, block_len, 0)
        allowed = allowed_pairs(query_start, group_len)
        scores = jnp.einsum("qhd,khd->hqk", queries, key_all, preferred_element_type=jnp.float32)
        masked = jnp.where(allowed[None], scores, NEGATIVE)
        row_top = jnp.max(masked, axis=2, keepdims=True)
        exponent = jnp.where(allowed[None], jnp.exp(masked - row_top), 0.0)
        denominator = jnp.sum(exponent, axis=2)
        numerator = jnp.einsum(
            "hqk,khd->qhd",
            exponent.astype(jnp.bfloat16),
            value_all,
            preferred_element_type=jnp.float32,
        )
        return (numerator / denominator.T[:, :, None]).astype(jnp.bfloat16)

    block_starts = jnp.arange(block_count, dtype=jnp.int32) * block_len
    heads_out = lax.map(query_block, block_starts).reshape(group_len, head_width)
    attn_rows = lax.psum_scatter(
        jnp.dot(heads_out, out_weight, preferred_element_type=jnp.float32).astype(jnp.bfloat16),
        "head",
        scatter_dimension=0,
        tiled=True,
    ).astype(jnp.float32)
    stream = (tokens.astype(jnp.float32) + attn_rows).reshape(local_rows // 4, 4, D)
    average = jnp.sum(stream, axis=2, keepdims=True) / D
    variance = jnp.sum(stream * stream, axis=2, keepdims=True) / D - average * average
    window_rows = ((stream - average) * lax.rsqrt(variance + EPSILON) * merge_gain).astype(
        jnp.bfloat16
    )
    merged_slice = lax.all_to_all(
        window_rows.reshape(local_rows // 4, 4 * D), "head", split_axis=1, concat_axis=0, tiled=True
    )
    merged_count = local_rows // 4
    column_terms = jnp.dot(
        merged_slice,
        lax.all_gather(merge_weight, "tok", axis=1, tiled=True),
        preferred_element_type=jnp.float32,
    )
    projected = lax.psum_scatter(
        column_terms.astype(jnp.bfloat16), "head", scatter_dimension=0, tiled=True
    )
    slot_count = max(2, 2 * merged_count // tok_count)
    owner_col = owners[:, 0]
    owner_hot = (owner_col[:, None] == jnp.arange(tok_count, dtype=jnp.int32)[None, :]).astype(
        jnp.int32
    )
    earlier = jnp.cumsum(owner_hot, axis=0, dtype=jnp.int32) - owner_hot
    slot_index = jnp.sum(earlier * owner_hot, axis=1, dtype=jnp.int32)
    target = owner_col * slot_count + slot_index
    select = (
        jnp.arange(tok_count * slot_count, dtype=jnp.int32)[:, None] == target[None, :]
    ).astype(jnp.bfloat16)
    send_rows = jnp.dot(select, projected, preferred_element_type=jnp.float32).astype(jnp.bfloat16)
    send_rows = send_rows.reshape(tok_count, slot_count, -1)
    received = lax.all_to_all(send_rows, "tok", split_axis=0, concat_axis=0, tiled=True)
    return received.reshape(tok_count * slot_count, -1)


def solution(mesh):
    placed = (
        P(("tok", "head"), None),
        P(),
        P(None, "head", None),
        P("head", None),
        P(),
        P("head", "tok"),
        P(None, "tok"),
        P("tok"),
        P(None, "tok"),
        P("tok"),
        P(("tok", "head"), None),
    )
    return jax.shard_map(
        body, mesh=mesh, in_specs=placed, out_specs=P(("tok", "head"), None), check_vma=False
    )
```

profile of v0, /device:TPU:57, one launch (start us, length us, event | category | flops | bytes accessed | tf_op | source)
XLA Modules:
  0.0 257.5 jit_solution(5983882378429077472)
XLA Ops:
  7.4 1.3 convert_reduce_fusion
  8.7 1.3 fusion.46
  10.0 2.1 fusion.48
  12.1 0.7 convert_element_type.65
  12.8 0.7 broadcast_subtract_fusion
  13.5 0.1 select_reduce_fusion.2
  13.6 0.8 convert_multiply_fusion.1
  14.4 0.7 broadcast_compare_fusion
  15.1 1.0 multiply_cosine_fusion.1
  16.1 28.8 %all-gather.3.cloned.1.call-done = bf16[1024,1664]{1,0:T(8,128)(2,1)} async-done(((bf16[128,1664]{1,0:T(8,128)(2,1)}), bf16[1024,1664]{1,0:T(8,128)(2,1)}) %all-gather.3.cloned.1.call-update) | async-done | bytes 3407888 | tf_op jit(solution)/shard_map/all_gather | solution.py:64
  44.9 4.5 %fusion.39 = f32[1024,3,2,104]{0,3,2,1:T(8,128)S(1)} fusion(bf16[3,2,104,1664]{3,2,1,0:T(8,128)(2,1)S(1)} %bitcast.70, bf16[1024,1664]{1,0:T(8,128)(2,1)} %all-gather.3.cloned.1.call-done), kind=kOutput, calls=%fused_computation.27 | convolution fusion | flops 2126512128 | bytes 8040448 | tf_op jit(solution)/shard_map/dot_general | solution.py:63
  49.4 0.2 slice_bitcast_fusion
  49.6 0.8 fusion.50
  50.4 0.2 subtract_convert_fusion.1
  50.6 0.2 multiply_subtract_fusion.1
  50.8 0.9 pad_maximum_fusion
  51.7 0.9 fusion.49
  52.6 23.1 %while.10 = (s32[]{:T(128)}, bf16[2,512,2,104]{1,3,2,0:T(8,128)(2,1)}, s32[2]{0:T(128)S(1)}, s32[1024]{0:T(1024)S(1)}, pred[1024]{0:T(1024)(128)(4,1)S(1)}, /*in...) while((s32[]{:T(128)}, ...), condition=%wide.region_9.10_spmd, body=%wide.region_6.0_spmd.sunk | while | flops 443762176 | bytes 7069351 | solution.py:103
  52.6 0.6 dynamic_slice.26
  55.1 0.1 dynamic_slice.27
  55.1 0.6 iota_add_fusion.2
  55.8 0.7 fusion.80
  56.4 4.6 %fusion.81 = (f32[2,512]{1,0:T(2,128)S(1)}, bf16[2,512,1024]{2,1,0:T(8,128)(2,1)}) fusion(pred[512,1024]{1,0:T(8,128)(4,1)S(1)} %fusion.80, bf16[1024,2,104]{0,2,1:T(8,128)(2,1)} %get-tuple-element.180, bf16[1024,2,104]{0,2,1:T(8,128)(2,1)} %get-tuple-element.179, s32[]{:T(128)S(6)} %select_n.34), kind=kOutput, calls=%fused_computation.84.clone.1 | convolution fusion | flops 223347712 | bytes 3788804 | tf_op jit(solution)/shard_map/while/body/eval_jaxpr/sub | solution.py:92
  61.0 3.1 %fusion.82 = bf16[2,512,2,104]{1,3,2,0:T(8,128)(2,1)} fusion(bf16[2,512,2,104]{1,3,2,0:T(8,128)(2,1)} %get-tuple-element.164, s32[]{:T(128)} %get-tuple-element.163, bf16[1024,2,104]{0,2,1:T(8,128)(2,1)} %get-tuple-element.181, bf16[2,512,1024]{2,1,0:T(8,128)(2,1)} %get-tuple-element.150, f32[512,2]{0,1:T(2,128)S(1)} %bitcast.80), kind=kOutput, calls=%fused_computation.15.clone.1 | convolution fusion | flops 218316800 | bytes 2740736 | tf_op jit(solution)/shard_map/while/body/eval_jaxpr/hqk,khd->qhd/dot_general | solution.py:94
  64.1 0.6 dynamic_slice.26
  66.7 0.6 iota_add_fusion.2
  67.3 0.7 fusion.80
  68.0 4.6 %fusion.81 = (f32[2,512]{1,0:T(2,128)S(1)}, bf16[2,512,1024]{2,1,0:T(8,128)(2,1)}) fusion(pred[512,1024]{1,0:T(8,128)(4,1)S(1)} %fusion.80, bf16[1024,2,104]{0,2,1:T(8,128)(2,1)} %get-tuple-element.180, bf16[1024,2,104]{0,2,1:T(8,128)(2,1)} %get-tuple-element.179, s32[]{:T(128)S(6)} %select_n.34), kind=kOutput, calls=%fused_computation.84.clone.1 | convolution fusion | flops 223347712 | bytes 3788804 | tf_op jit(solution)/shard_map/while/body/eval_jaxpr/sub | solution.py:92
  72.6 3.1 %fusion.82 = bf16[2,512,2,104]{1,3,2,0:T(8,128)(2,1)} fusion(bf16[2,512,2,104]{1,3,2,0:T(8,128)(2,1)} %get-tuple-element.164, s32[]{:T(128)} %get-tuple-element.163, bf16[1024,2,104]{0,2,1:T(8,128)(2,1)} %get-tuple-element.181, bf16[2,512,1024]{2,1,0:T(8,128)(2,1)} %get-tuple-element.150, f32[512,2]{0,1:T(2,128)S(1)} %bitcast.80), kind=kOutput, calls=%fused_computation.15.clone.1 | convolution fusion | flops 218316800 | bytes 2740736 | tf_op jit(solution)/shard_map/while/body/eval_jaxpr/hqk,khd->qhd/dot_general | solution.py:94
  75.7 1.4 copy.16
  77.2 3.0 %convolution_convert_fusion.2 = bf16[1024,1664]{1,0:T(8,128)(2,1)} fusion(bf16[1024,208]{0,1:T(8,128)(2,1)S(1)} %bitcast.71, bf16[208,1664]{1,0:T(8,128)(2,1)S(1)} %copy-done.2), kind=kOutput, calls=%fused_computation.26 | convolution fusion | flops 710541312 | bytes 4526080 | tf_op jit(solution)/shard_map/dot_general | solution.py:105
  80.3 0.5 all-gather.5.cloned.1.call-update
  80.9 0.1 mul.313
  81.0 38.2 %reduce-scatter.3.cloned.1.call-done = bf16[128,1664]{1,0:T(8,128)(2,1)} async-done(((bf16[1024,1664]{1,0:T(8,128)(2,1)}), bf16[128,1664]{1,0:T(8,128)(2,1)}) %reduce-scatter.3.cloned.1.call-update) | async-done | bytes 426000 | tf_op jit(solution)/shard_map/reduce_scatter | solution.py:104
  119.2 2.1 fusion.53
  121.3 0.1 div.50
  121.4 0.1 div.52
  121.7 1.4 reshape.306
  123.1 0.3 fusion.45
  123.4 11.3 %all_to_all.21 = bf16[32,8,832]{2,0,1:T(8,128)(2,1)S(1)} all-to-all(bf16[32,8,832]{2,0,1:T(8,128)(2,1)S(1)} %fusion.45), channel_id=1, replica_groups=mesh['tok'=32,'head'=8] {'head'}, dimensions={1} | all-to-all | bytes 851968 | tf_op jit(solution)/shard_map/all_to_all | solution.py:116
  134.7 39.1 %all-gather.5.cloned.1.call-done = bf16[832,4096]{1,0:T(8,128)(2,1)} async-done(((bf16[832,128]{1,0:T(8,128)(2,1)}), bf16[832,4096]{1,0:T(8,128)(2,1)}) %all-gather.5.cloned.1.call-update) | async-done | bytes 6815760 | tf_op jit(solution)/shard_map/all_gather | solution.py:122
  173.8 6.8 %convolution_convert_fusion = bf16[256,4096]{1,0:T(8,128)(2,1)} fusion(bf16[256,832]{1,0:T(8,128)(2,1)S(1)} %bitcast.73, bf16[832,4096]{1,0:T(8,128)(2,1)} %all-gather.5.cloned.1.call-done), kind=kOutput, calls=%fused_computation.24 | convolution fusion | flops 1745879040 | bytes 9338880 | tf_op jit(solution)/shard_map/dot_general | solution.py:120
  180.7 0.2 select_reduce_fusion.3
  180.9 39.6 %reduce-scatter.5.cloned.1.call-done = bf16[32,4096]{1,0:T(8,128)(2,1)} async-done(((bf16[256,4096]{1,0:T(8,128)(2,1)}), bf16[32,4096]{1,0:T(8,128)(2,1)}) %reduce-scatter.5.cloned.1.call-update) | async-done | bytes 262160 | tf_op jit(solution)/shard_map/reduce_scatter | solution.py:125
  220.5 1.2 convolution_convert_fusion.1
  221.7 0.3 reshape.307
  222.1 27.3 %all_to_all.22 = bf16[32,2,4096]{2,1,0:T(2,128)(2,1)S(1)} all-to-all(bf16[32,2,4096]{2,1,0:T(2,128)(2,1)S(1)} %reshape.307), channel_id=1, replica_groups=mesh['tok'=32,'head'=8] {'tok'}, dimensions={0} | all-to-all | bytes 1048576 | tf_op jit(solution)/shard_map/all_to_all | solution.py:141
  249.4 1.0 reshape.308
  (40 shorter events, 0.8 us)
Async XLA Ops:
  7.4 37.5 %copy-start = (bf16[3,208,1664]{2,1,0:T(8,128)(2,1)S(1)}, bf16[3,208,1664]{2,1,0:T(8,128)(2,1)}, u32[]{:S(2)}) copy-start(bf16[3,208,1664]{2,1,0:T(8,128)(2,1)} %param.15) | copy-start | bytes 6230020
  7.4 37.5 %all-gather.3.cloned.1.call-start = ((), (), s32[]{:S(2)}) async-start(), calls=%async_computation.4 | async-start | bytes 3833856 | tf_op jit(solution)/shard_map/all_gather | solution.py:64
  12.1 107.1 %reduce-scatter.3.cloned.1.call-start = ((), (), s32[]{:S(2)}) async-start(), calls=%async_computation.5 | async-start | bytes 3833856 | tf_op jit(solution)/shard_map/reduce_scatter | solution.py:104
  50.4 2.2 copy-start.3
  52.6 24.6 %copy-start.2 = (bf16[208,1664]{1,0:T(8,128)(2,1)S(1)}, bf16[208,1664]{1,0:T(8,128)(2,1)}, u32[]{:S(2)}) copy-start(bf16[208,1664]{1,0:T(8,128)(2,1)} %param.16) | copy-start | bytes 2076676
  80.2 0.7 copy-start.4
  80.2 39.0 %copy-start.1 = (bf16[128,1664]{1,0:T(8,128)(2,1)S(1)}, bf16[128,1664]{1,0:T(8,128)(2,1)}, u32[]{:S(2)}) copy-start(bf16[128,1664]{1,0:T(8,128)(2,1)} %param.13) | copy-start | bytes 1277956
  80.2 93.6 %all-gather.5.cloned.1.call-start = ((), (), s32[]{:S(2)}) async-start(), calls=%async_computation.6 | async-start | bytes 7028736 | tf_op jit(solution)/shard_map/all_gather | solution.py:122
  80.8 139.7 %reduce-scatter.5.cloned.1.call-start = ((), (), s32[]{:S(2)}) async-start(), calls=%async_computation.7 | async-start | bytes 2359296 | tf_op jit(solution)/shard_map/reduce_scatter | solution.py:125
  173.8 6.8 %copy-start.5 = (s32[32,1]{0,1:T(1,128)S(1)}, s32[32,1]{0,1:T(1,128)}, u32[]{:S(2)}) copy-start(s32[32,1]{0,1:T(1,128)} %param.23) | copy-start | bytes 388
Sparse Core Ops, SparseCore 0:
  12.2 32.6 all-gather.2
  80.3 38.8 reduce-scatter.2
  180.7 39.7 reduce-scatter.4
Sparse Core Ops, SparseCore 1:
  83.2 90.5 all-gather.4
where the time goes:
time: 258 us; the launch traced here: 257 us
  waiting for transfers between devices  146 us (57%)
  blocking collectives  38.6 us (15%)
  matrix products  30.8 us (12%)
  other arithmetic  16.1 us (6%)
  between operations  14.7 us (6%)
  local copies, waits for them, and re-layouts  7.14 us (3%)
  loops' own time  3.76 us (1%)
    reduce_scatter x1, waiting for transfers between devices, body(): lax.psum_scatter(column_terms.astype(jnp.bfloat16), 'head', scatter_dimen...  39.6 us
    all_gather x1, waiting for transfers between devices, body(): lax.all_gather(merge_weight, 'tok', axis=1, tiled=True)  39.1 us
    reduce_scatter x1, waiting for transfers between devices, body(): lax.psum_scatter(jnp.dot(heads_out, out_weight, preferred_element_type=jn...  38.2 us
    all_gather x1, waiting for transfers between devices, body(): lax.all_gather(normed, 'head', axis=0, tiled=True)  28.8 us
    all_to_all x1, blocking collectives, body(): lax.all_to_all(send_rows, 'tok', split_axis=0, concat_axis=0, tiled=True)  27.3 us
    all_to_all x1, blocking collectives, body(): lax.all_to_all(window_rows.reshape(local_rows // 4, 4 * D), 'head', split...  11.3 us
    sub x2, matrix products, query_block(): exponent = jnp.where(allowed[None], jnp.exp(masked - row_top), 0.0)  9.22 us
    dot_general x1, matrix products, body(): jnp.dot(merged_slice, lax.all_gather(merge_weight, 'tok', axis=1, tiled=T...  6.76 us
  transfers between devices with their start and end apart: 4, of which 4 were waited for; matrix products, arithmetic and copies ran while one was open for 3% of the time, Pallas kernels for 0%

commit v1 on v0

--- a/solution.py
+++ b/solution.py
@@ -61,7 +61,10 @@
     stacked_weight = qkv_weight.reshape(3 * head_width, D)
     normed = layer_norm(tokens.astype(jnp.float32), attn_gain).astype(jnp.bfloat16)
     projected_rows = lax.dot_general(
-        lax.all_gather(normed, "head", axis=0, tiled=True),
+        jnp.concatenate(
+            lax.all_to_all(jnp.stack(lax.axis_size("head") * [normed], axis=0), "head", 0, 0),
+            axis=0,
+        ),
         stacked_weight,
         (((1,), (1,)), ((), ())),
         preferred_element_type=jnp.float32,

time: 258 us -> 273 us (1.058)
  waiting for transfers between devices: 146 us -> 156 us
  starting transfers between devices: 0.13 us -> 5.2 us
  other arithmetic: 16.1 us -> 12.6 us
    all_to_all x0 -> x1, waiting for transfers between devices: none -> 37.4 us  [body(): lax.all_to_all(jnp.stack(lax.axis_size('head') * [normed], axis=0), 'head...]
    all_gather x1 -> x0, waiting for transfers between devices: 28.8 us -> none  [body(): lax.all_gather(normed, 'head', axis=0, tiled=True)]
    all_to_all x0 -> x1, starting transfers between devices: none -> 5.12 us  [body(): lax.all_to_all(jnp.stack(lax.axis_size('head') * [normed], axis=0), 'head...]
  transfers between devices with their start and end apart: 4 -> 4, of which waited for: 4 -> 4; matrix products, arithmetic and copies ran while one was open for 3% -> 2% of each run, Pallas kernels for 0% -> 0%
where the time goes in v1:
time: 273 us; the launch traced here: 272 us
  waiting for transfers between devices  156 us (57%)
  blocking collectives  38.5 us (14%)
  matrix products  30.9 us (11%)
  between operations  15.1 us (6%)
  other arithmetic  12.6 us (5%)
  local copies, waits for them, and re-layouts  9.29 us (3%)
  starting transfers between devices  5.2 us (2%)
  loops' own time  4.18 us (2%)
    reduce_scatter x1, waiting for transfers between devices, body(): lax.psum_scatter(jnp.dot(heads_out, out_weight, preferred_element_type=jn...  39.7 us
    reduce_scatter x1, waiting for transfers between devices, body(): lax.psum_scatter(column_terms.astype(jnp.bfloat16), 'head', scatter_dimen...  39.6 us
    all_gather x1, waiting for transfers between devices, body(): lax.all_gather(merge_weight, 'tok', axis=1, tiled=True)  39.1 us
    all_to_all x1, waiting for transfers between devices, body(): lax.all_to_all(jnp.stack(lax.axis_size('head') * [normed], axis=0), 'head...  37.4 us
    all_to_all x1, blocking collectives, body(): lax.all_to_all(send_rows, 'tok', split_axis=0, concat_axis=0, tiled=True)  27.2 us
    all_to_all x1, blocking collectives, body(): lax.all_to_all(window_rows.reshape(local_rows // 4, 4 * D), 'head', split...  11.2 us
    sub x2, matrix products, query_block(): exponent = jnp.where(allowed[None], jnp.exp(masked - row_top), 0.0)  9.23 us
    dot_general x1, matrix products, body(): jnp.dot(merged_slice, lax.all_gather(merge_weight, 'tok', axis=1, tiled=T...  6.76 us
  transfers between devices with their start and end apart: 4, of which 4 were waited for; matrix products, arithmetic and copies ran while one was open for 2% of the time, Pallas kernels for 0%

profile of v1, /device:TPU:57, one launch (start us, length us, event | category | flops | bytes accessed | tf_op | source)
XLA Modules:
  0.0 272.1 jit_solution(9222613179299946320)
XLA Ops:
  7.4 1.3 convert_reduce_fusion
  8.7 1.3 fusion.44
  9.9 1.3 fusion.46
  11.3 2.0 stack.2
  13.3 5.1 %all-to-all-start = ((bf16[8,128,1664]{2,1,0:T(8,128)(2,1)}), bf16[8,128,1664]{2,1,0:T(8,128)(2,1)}, u32[]{:S(2)}, u32[]{:S(2)}) async-start(bf16[8,128,1664]{2,1,0:T(8,128)(2,1)} %stack.2), calls=%async_computation | async-start | bytes 6815744 | tf_op jit(solution)/shard_map/all_to_all | solution.py:65
  18.5 0.1 select_reduce_fusion.2
  18.7 1.0 multiply_cosine_fusion.1
  19.7 37.4 %all-to-all-done = bf16[8,128,1664]{2,1,0:T(8,128)(2,1)} async-done(((bf16[8,128,1664]{2,1,0:T(8,128)(2,1)}), bf16[8,128,1664]{2,1,0:T(8,128)(2,1)}, u32[]{:S(2)}, u32[]{:S(2)}) %all-to-all-start) | async-done | bytes 3407904 | tf_op jit(solution)/shard_map/all_to_all | solution.py:65
  57.1 4.5 %fusion.57 = f32[1024,3,2,104]{0,3,2,1:T(8,128)S(1)} fusion(bf16[1024,1664,1,1]{1,0,3,2:T(8,128)(2,1)} %bitcast.7, bf16[3,2,104,1664]{3,2,1,0:T(8,128)(2,1)S(1)} %bitcast.71), kind=kOutput, calls=%fused_computation.83 | convolution fusion | flops 2126512128 | bytes 8040448 | tf_op jit(solution)/shard_map/dot_general | solution.py:63
  61.6 0.2 slice_bitcast_fusion
  61.8 0.8 fusion.48
  62.6 0.2 subtract_convert_fusion.1
  62.8 0.2 multiply_subtract_fusion.1
  63.0 0.9 pad_maximum_fusion
  63.9 0.9 fusion.47
  64.8 23.8 %while.10 = (s32[]{:T(128)}, bf16[2,512,2,104]{1,3,2,0:T(8,128)(2,1)}, s32[2]{0:T(128)S(1)}, s32[1024]{0:T(1024)S(1)}, pred[1024]{0:T(1024)(128)(4,1)S(1)}, /*in...) while((s32[]{:T(128)}, ...), condition=%wide.region_9.10_spmd, body=%wide.region_6.0_spmd.sunk | while | flops 443762176 | bytes 7069351 | solution.py:106
  64.8 0.7 dynamic_slice.26
  67.5 0.1 dynamic_slice.27
  67.6 0.7 iota_add_fusion.2
  68.3 0.7 fusion.80
  69.0 4.6 %fusion.81 = (f32[2,512]{1,0:T(2,128)S(1)}, bf16[2,512,1024]{2,1,0:T(8,128)(2,1)}) fusion(pred[512,1024]{1,0:T(8,128)(4,1)S(1)} %fusion.80, bf16[1024,2,104]{0,2,1:T(8,128)(2,1)} %get-tuple-element.180, bf16[1024,2,104]{0,2,1:T(8,128)(2,1)} %get-tuple-element.179, s32[]{:T(128)S(6)} %select_n.34), kind=kOutput, calls=%fused_computation.82.clone.1 | convolution fusion | flops 223347712 | bytes 3788804 | tf_op jit(solution)/shard_map/while/body/eval_jaxpr/sub | solution.py:95
  73.6 3.1 %fusion.82 = bf16[2,512,2,104]{1,3,2,0:T(8,128)(2,1)} fusion(bf16[2,512,2,104]{1,3,2,0:T(8,128)(2,1)} %get-tuple-element.164, s32[]{:T(128)} %get-tuple-element.163, bf16[1024,2,104]{0,2,1:T(8,128)(2,1)} %get-tuple-element.181, bf16[2,512,1024]{2,1,0:T(8,128)(2,1)} %get-tuple-element.150, f32[512,2]{0,1:T(2,128)S(1)} %bitcast.81), kind=kOutput, calls=%fused_computation.15.clone.1 | convolution fusion | flops 218316800 | bytes 2740736 | tf_op jit(solution)/shard_map/while/body/eval_jaxpr/hqk,khd->qhd/dot_general | solution.py:97
  76.7 0.7 dynamic_slice.26
  79.4 0.1 dynamic_slice.27
  79.5 0.7 iota_add_fusion.2
  80.2 0.7 fusion.80
  80.9 4.6 %fusion.81 = (f32[2,512]{1,0:T(2,128)S(1)}, bf16[2,512,1024]{2,1,0:T(8,128)(2,1)}) fusion(pred[512,1024]{1,0:T(8,128)(4,1)S(1)} %fusion.80, bf16[1024,2,104]{0,2,1:T(8,128)(2,1)} %get-tuple-element.180, bf16[1024,2,104]{0,2,1:T(8,128)(2,1)} %get-tuple-element.179, s32[]{:T(128)S(6)} %select_n.34), kind=kOutput, calls=%fused_computation.82.clone.1 | convolution fusion | flops 223347712 | bytes 3788804 | tf_op jit(solution)/shard_map/while/body/eval_jaxpr/sub | solution.py:95
  85.5 3.1 %fusion.82 = bf16[2,512,2,104]{1,3,2,0:T(8,128)(2,1)} fusion(bf16[2,512,2,104]{1,3,2,0:T(8,128)(2,1)} %get-tuple-element.164, s32[]{:T(128)} %get-tuple-element.163, bf16[1024,2,104]{0,2,1:T(8,128)(2,1)} %get-tuple-element.181, bf16[2,512,1024]{2,1,0:T(8,128)(2,1)} %get-tuple-element.150, f32[512,2]{0,1:T(2,128)S(1)} %bitcast.81), kind=kOutput, calls=%fused_computation.15.clone.1 | convolution fusion | flops 218316800 | bytes 2740736 | tf_op jit(solution)/shard_map/while/body/eval_jaxpr/hqk,khd->qhd/dot_general | solution.py:97
  88.6 1.4 copy.16
  90.1 3.0 %convolution_convert_fusion.2 = bf16[1024,1664]{1,0:T(8,128)(2,1)} fusion(bf16[1024,208]{0,1:T(8,128)(2,1)S(1)} %bitcast.72, bf16[208,1664]{1,0:T(8,128)(2,1)S(1)} %copy-done.2), kind=kOutput, calls=%fused_computation.26 | convolution fusion | flops 710541312 | bytes 4526080 | tf_op jit(solution)/shard_map/dot_general | solution.py:108
  93.1 0.5 all-gather.2.cloned.1.call-update
  93.8 0.1 mul.313
  93.9 39.7 %reduce-scatter.3.cloned.1.call-done = bf16[128,1664]{1,0:T(8,128)(2,1)} async-done(((bf16[1024,1664]{1,0:T(8,128)(2,1)}), bf16[128,1664]{1,0:T(8,128)(2,1)}) %reduce-scatter.3.cloned.1.call-update) | async-done | bytes 426000 | tf_op jit(solution)/shard_map/reduce_scatter | solution.py:107
  133.6 2.1 fusion.51
  135.7 0.1 div.50
  135.8 0.1 div.52
  135.9 0.1 copy.17
  136.1 1.4 reshape.312
  137.5 0.3 fusion.43
  137.9 11.2 %all_to_all.26 = bf16[32,8,832]{2,0,1:T(8,128)(2,1)S(1)} all-to-all(bf16[32,8,832]{2,0,1:T(8,128)(2,1)S(1)} %fusion.43), channel_id=1, replica_groups=mesh['tok'=32,'head'=8] {'head'}, dimensions={1} | all-to-all | bytes 851968 | tf_op jit(solution)/shard_map/all_to_all | solution.py:119
  149.1 39.1 %all-gather.2.cloned.1.call-done = bf16[832,4096]{1,0:T(8,128)(2,1)} async-done(((bf16[832,128]{1,0:T(8,128)(2,1)}), bf16[832,4096]{1,0:T(8,128)(2,1)}) %all-gather.2.cloned.1.call-update) | async-done | bytes 6815760 | tf_op jit(solution)/shard_map/all_gather | solution.py:125
  188.2 6.8 %convolution_convert_fusion = bf16[256,4096]{1,0:T(8,128)(2,1)} fusion(bf16[256,832]{1,0:T(8,128)(2,1)S(1)} %bitcast.74, bf16[832,4096]{1,0:T(8,128)(2,1)} %all-gather.2.cloned.1.call-done), kind=kOutput, calls=%fused_computation.24 | convolution fusion | flops 1745879040 | bytes 9338880 | tf_op jit(solution)/shard_map/dot_general | solution.py:123
  195.1 0.2 select_reduce_fusion.3
  195.3 39.6 %reduce-scatter.5.cloned.1.call-done = bf16[32,4096]{1,0:T(8,128)(2,1)} async-done(((bf16[256,4096]{1,0:T(8,128)(2,1)}), bf16[32,4096]{1,0:T(8,128)(2,1)}) %reduce-scatter.5.cloned.1.call-update) | async-done | bytes 262160 | tf_op jit(solution)/shard_map/reduce_scatter | solution.py:128
  234.9 1.2 convolution_convert_fusion.1
  236.1 0.3 reshape.313
  236.5 27.2 %all_to_all.27 = bf16[32,2,4096]{2,1,0:T(2,128)(2,1)S(1)} all-to-all(bf16[32,2,4096]{2,1,0:T(2,128)(2,1)S(1)} %reshape.313), channel_id=1, replica_groups=mesh['tok'=32,'head'=8] {'tok'}, dimensions={0} | all-to-all | bytes 1048576 | tf_op jit(solution)/shard_map/all_to_all | solution.py:144
  263.7 1.0 reshape.314
  (46 shorter events, 0.6 us)
Async XLA Ops:
  7.4 49.7 %copy-start = (bf16[3,208,1664]{2,1,0:T(8,128)(2,1)S(1)}, bf16[3,208,1664]{2,1,0:T(8,128)(2,1)}, u32[]{:S(2)}) copy-start(bf16[3,208,1664]{2,1,0:T(8,128)(2,1)} %param.15) | copy-start | bytes 6230020
  13.3 5.1 %copy-start.8 = (s32[2,4]{1,0:T(2,128)S(1)}, s32[2,4]{1,0:T(2,128)}, u32[]{:S(2)}) copy-start(s32[2,4]{1,0:T(2,128)} %param.19) | copy-start | bytes 100
  13.3 5.2 %copy-start.3 = (s32[1024]{0:T(1024)S(1)}, s32[1024]{0:T(1024)}, u32[]{:S(2)}) copy-start(s32[1024]{0:T(1024)} %param.20) | copy-start | bytes 12292
  13.3 5.3 %copy-start.4 = (s32[2,1024]{1,0:T(2,128)S(1)}, s32[2,1024]{1,0:T(2,128)}, u32[]{:S(2)}) copy-start(s32[2,1024]{1,0:T(2,128)} %param.21) | copy-start | bytes 24580
  13.3 5.4 %copy-start.6 = (s32[1024]{0:T(1024)S(1)}, s32[1024]{0:T(1024)}, u32[]{:S(2)}) copy-start(s32[1024]{0:T(1024)} %param.22) | copy-start | bytes 12292
  13.3 43.8 %all-to-all-start = ((bf16[8,128,1664]{2,1,0:T(8,128)(2,1)}), bf16[8,128,1664]{2,1,0:T(8,128)(2,1)}, u32[]{:S(2)}, u32[]{:S(2)}) async-start(bf16[8,128,1664]{2,1,0:T(8,128)(2,1)} %stack.2), calls=%async_computation | async-start | bytes 6815744 | tf_op jit(solution)/shard_map/all_to_all | solution.py:65
  18.4 115.2 %reduce-scatter.3.cloned.1.call-start = ((), (), s32[]{:S(2)}) async-start(), calls=%async_computation.5 | async-start | bytes 3833856 | tf_op jit(solution)/shard_map/reduce_scatter | solution.py:107
  64.8 25.3 %copy-start.2 = (bf16[208,1664]{1,0:T(8,128)(2,1)S(1)}, bf16[208,1664]{1,0:T(8,128)(2,1)}, u32[]{:S(2)}) copy-start(bf16[208,1664]{1,0:T(8,128)(2,1)} %param.16) | copy-start | bytes 2076676
  93.1 0.7 copy-start.5
  93.1 40.5 %copy-start.1 = (bf16[128,1664]{1,0:T(8,128)(2,1)S(1)}, bf16[128,1664]{1,0:T(8,128)(2,1)}, u32[]{:S(2)}) copy-start(bf16[128,1664]{1,0:T(8,128)(2,1)} %param.13) | copy-start | bytes 1277956
  93.1 95.1 %all-gather.2.cloned.1.call-start = ((), (), s32[]{:S(2)}) async-start(), calls=%async_computation.6 | async-start | bytes 7028736 | tf_op jit(solution)/shard_map/all_gather | solution.py:125
  93.7 141.2 %reduce-scatter.5.cloned.1.call-start = ((), (), s32[]{:S(2)}) async-start(), calls=%async_computation.7 | async-start | bytes 2359296 | tf_op jit(solution)/shard_map/reduce_scatter | solution.py:128
  188.2 6.8 %copy-start.7 = (s32[32,1]{0,1:T(1,128)S(1)}, s32[32,1]{0,1:T(1,128)}, u32[]{:S(2)}) copy-start(s32[32,1]{0,1:T(1,128)} %param.23) | copy-start | bytes 388
Sparse Core Ops, SparseCore 0:
  93.2 40.3 reduce-scatter.2
  195.1 39.7 reduce-scatter.4
Sparse Core Ops, SparseCore 1:
  96.0 92.1 all-gather.1
